TPU v7x, 128 devices: a whole 4x4x4 slice. The times are simulated.
128 devices in a mesh: leaf: 4 (over x), row: 2 (over core), col: 16 (over z, y).
Axes of the slice: x: 4, y: 4, z: 4, core: 2. Of those that a mesh axis runs over, the one named last changes fastest.
Arguments:
- sec_rhs: float32 [4, 7, 64, 2048], P('leaf', None, None, 'row'), may hold values from -6 to 6
- sec_inv: float32 [4, 7, 2048, 2048], P('leaf', None, 'row', 'col'), as said below
- sec_low: float32 [4, 10, 2048, 2048], P('leaf', None, 'row', 'col'), may hold values from -0.09375 to 0.09375
- sec_top: float32 [4, 7, 2048, 2048], P('leaf', None, 'row', 'col'), may hold values from -0.046875 to 0.046875
- sec_rows: int32 [4, 7, 16], P('leaf'), may hold values from 0 to 47, as said below
- top_rhs: float32 [7, 64, 2048], P(None, None, 'row'), may hold values from -6 to 6
- top_inv: float32 [7, 2048, 2048], P(None, 'row', 'col'), as said below
- top_low: float32 [10, 2048, 2048], P(None, 'row', 'col'), may hold values from -0.09375 to 0.09375
- sec_parent: int32 [4], replicated, may hold values from 0 to 3, as said below
- top_parent: int32 [4], replicated, may hold values from 0 to 1, as said below
Outputs:
- sec_sol: float32 [4, 7, 64, 2048], P('leaf', None, None, 'row')
- top_sol: float32 [7, 64, 2048], P(None, None, 'row')
Inputs may be any that keep to these rules, and one draw needn't show every extreme that they name: `sec_rows`: within each list the 16 values are distinct. `sec_parent`: each of 0, 1, 2, 3 appears exactly once. `top_parent`: each of 0 and 1 appears exactly twice. `sec_inv`: dense matrices with a positive diagonal; nothing more is promised of their entries. `top_inv`: dense matrices with a positive diagonal; nothing more is promised of their entries.
All inputs are finite; a program needn't handle non-finite values.
Results may differ from a plain program's by a relative error of at most 0.00012.
Values sent between devices are 32-bit elements; how exact they have to be, the bound alone decides.
No kernel may reach another device: no remote copies, remote signals or barrier semaphores. Data moves between devices by JAX's collectives and lax.ppermute only.
A program may use at most 128 MiB of HBM per device.

v0:
```python
import jax
import jax.numpy as jnp
from jax import lax
from jax.sharding import PartitionSpec as P

BLOCK = 128


def apply_block(vectors, matrices):
    return jnp.einsum("btc,brc->btr", vectors, matrices, precision=lax.Precision.HIGHEST)


def per_device(
    sec_rhs, sec_inv, sec_low, sec_top, sec_rows, top_rhs, top_inv, top_low, sec_parent, top_parent
):
    parts_row = lax.axis_size("row")
    here_row = lax.axis_index("row")
    here_col = lax.axis_index("col")
    here_leaf = lax.axis_index("leaf")
    rows_here = sec_rhs.shape[-1]
    cols_here = sec_inv.shape[-1]
    width = rows_here * parts_row
    blocks = width // BLOCK
    nrhs = sec_rhs.shape[2]

    def own_cols(full):
        return lax.dynamic_slice_in_dim(full, here_col * cols_here, cols_here, 2)

    def solve_level(known, partial_value, inverse):
        if partial_value is None:
            y_rows = known
        else:
            y_rows = known - lax.psum(partial_value, "col")
        y_full = lax.all_gather(y_rows, "row", axis=2, tiled=True)
        x_part = apply_block(own_cols(y_full), inverse)
        x_rows = lax.psum(x_part, "col")
        x_full = lax.all_gather(x_rows, "row", axis=2, tiled=True)
        return (x_rows, x_full)

    right_side = sec_rhs[0]
    inverse = sec_inv[0]
    lower = sec_low[0]
    rows_leaf, full_leaf = solve_level(right_side[0:4], None, inverse[0:4])
    cols_leaf = own_cols(full_leaf)
    upward = apply_block(cols_leaf, lower[0:4])
    acc_mid = upward.reshape(2, 2, nrhs, rows_here).sum(1)
    acc_root = apply_block(cols_leaf, lower[4:8]).sum(0, keepdims=True)
    rows_mid, full_mid = solve_level(right_side[4:6], acc_mid, inverse[4:6])
    cols_mid = own_cols(full_mid)
    acc_root = acc_root + apply_block(cols_mid, lower[8:10]).sum(0, keepdims=True)
    rows_root, full_root = solve_level(right_side[6:7], acc_root, inverse[6:7])
    sec_out = jnp.concatenate([rows_leaf, rows_mid, rows_root], axis=0)[None]
    all_cols = jnp.concatenate([cols_leaf, cols_mid, own_cols(full_root)], axis=0)
    block_rows = sec_top.shape[2] // BLOCK
    contrib = apply_block(all_cols, sec_top[0]).reshape(7, nrhs, block_rows, BLOCK)
    mine = lax.dynamic_slice_in_dim(sec_rows[0], here_row * block_rows, block_rows, 1)
    section_ids = jnp.arange(sec_parent.shape[0], dtype=jnp.int32)
    parent_node = jnp.sum(jnp.where(section_ids == here_leaf, sec_parent, 0))
    grand_node = jnp.sum(jnp.where(jnp.arange(4, dtype=jnp.int32) == parent_node, top_parent, 0))
    path_which = mine // blocks
    node_of = jnp.where(path_which == 0, parent_node, jnp.where(path_which == 1, grand_node + 4, 6))
    sub_block = mine % blocks
    node_ids = jnp.arange(7, dtype=jnp.int32)
    block_ids = jnp.arange(blocks, dtype=jnp.int32)
    one_hot = (
        (node_of[:, :, None, None] == node_ids[None, None, :, None])
        & (sub_block[:, :, None, None] == block_ids[None, None, None, :])
    ).astype(jnp.float32)
    one_hot = one_hot.reshape(7, block_rows, 7, parts_row, blocks // parts_row)
    spread = jnp.einsum("jtkl,jknpm->pntml", contrib, one_hot, precision=lax.Precision.HIGHEST)
    spread = spread.reshape(parts_row, 7, nrhs, rows_here)
    total_update = lax.psum(spread, ("leaf", "row", "col"))
    top_update = lax.dynamic_index_in_dim(total_update, here_row, 0, keepdims=False)
    known_top = top_rhs - top_update
    earlier = jnp.sum(((sec_parent == parent_node) & (section_ids < here_leaf)).astype(jnp.int32))
    owner = (earlier == 0).astype(jnp.float32)
    known_own = lax.dynamic_slice_in_dim(known_top, parent_node, 1, 0)
    inverse_own = lax.dynamic_slice_in_dim(top_inv, parent_node, 1, 0)
    rows_own, full_own = solve_level(known_own, None, inverse_own)
    lower_pair = lax.dynamic_slice_in_dim(top_low, 2 * parent_node, 2, 0)
    reaches = jnp.einsum(
        "tc,brc->btr", own_cols(full_own)[0], lower_pair, precision=lax.Precision.HIGHEST
    )
    mid_hot = (jnp.arange(2, dtype=jnp.int32) == grand_node).astype(jnp.float32)
    slot_hot = (jnp.arange(4, dtype=jnp.int32) == parent_node).astype(jnp.float32)
    sol_term = slot_hot[:, None, None] * rows_own * owner
    mid_term = mid_hot[:, None, None] * reaches[0:1] * owner
    root_term = reaches[1:2] * owner
    rows_three, acc_four, acc_top = lax.psum((sol_term, mid_term, root_term), "leaf")
    rows_four, full_four = solve_level(known_top[4:6], acc_four, top_inv[4:6])
    acc_top = acc_top + apply_block(own_cols(full_four), top_low[8:10]).sum(0, keepdims=True)
    rows_five, full_five = solve_level(known_top[6:7], acc_top, top_inv[6:7])
    top_out = jnp.concatenate([rows_three, rows_four, rows_five], axis=0)
    return (sec_out, top_out)


def solution(mesh):
    placed = (
        P("leaf", None, None, "row"),
        P("leaf", None, "row", "col"),
        P("leaf", None, "row", "col"),
        P("leaf", None, "row", "col"),
        P("leaf", None, None),
        P(None, None, "row"),
        P(None, "row", "col"),
        P(None, "row", "col"),
        P(),
        P(),
    )
    return jax.shard_map(
        per_device,
        mesh=mesh,
        in_specs=placed,
        out_specs=(P("leaf", None, None, "row"), P(None, None, "row")),
        check_vma=False,
    )
```

profile of v0, /device:TPU:0, one launch (start us, length us, event | category | flops | bytes accessed | tf_op | source)
XLA Modules:
  0.0 1243.3 jit_solution(16419535620356213125)
XLA Ops:
  7.2 2.3 slice.73
  9.6 16.4 %all-gather.18.cloned.1.call-done = f32[1,4,64,2048]{3,2,1,0:T(8,128)} async-done(((f32[1,4,64,1024]{3,2,1,0:T(8,128)}), f32[1,4,64,2048]{3,2,1,0:T(8,128)}) %all-gather.18.cloned.1.call-update) | async-done | bytes 2097168 | tf_op jit(solution)/shard_map/all_gather | solution.py:34
  26.0 5.0 fusion.6
  31.1 88.9 %all-reduce.14.cloned.1.call-done = f32[4,64,1024]{2,1,0:T(8,128)} async-done(((f32[4,64,1024]{2,1,0:T(8,128)}), f32[4,64,1024]{2,1,0:T(8,128)}) %all-reduce.14.cloned.1.call-update) | async-done | bytes 1048592 | tf_op jit(solution)/shard_map/psum | solution.py:36
  120.1 14.1 %all-gather.8.cloned.1.call-done = f32[4,64,2048]{2,1,0:T(8,128)} async-done(((f32[4,64,1024]{2,1,0:T(8,128)}), f32[4,64,2048]{2,1,0:T(8,128)}) %all-gather.8.cloned.1.call-update) | async-done | bytes 2097168 | tf_op jit(solution)/shard_map/all_gather | solution.py:37
  135.1 4.8 bitcast_reduce_fusion
  140.0 87.2 %all-reduce.16.cloned.1.call-done = f32[2,64,1024]{2,1,0:T(8,128)} async-done(((f32[2,64,1024]{2,1,0:T(8,128)}), f32[2,64,1024]{2,1,0:T(8,128)}) %all-reduce.16.cloned.1.call-update) | async-done | bytes 524304 | tf_op jit(solution)/shard_map/psum | solution.py:33
  227.2 2.1 bitcast_subtract_fusion.1
  229.3 11.1 all-gather.10.cloned.1.call-done
  240.5 3.3 fusion.18
  243.8 87.4 %all-reduce.18.cloned.1.call-done = f32[2,64,1024]{2,1,0:T(8,128)} async-done(((f32[2,64,1024]{2,1,0:T(8,128)}), f32[2,64,1024]{2,1,0:T(8,128)}) %all-reduce.18.cloned.1.call-update) | async-done | bytes 524304 | tf_op jit(solution)/shard_map/psum | solution.py:36
  332.0 1.3 fusion.67
  334.0 3.7 fusion.12
  337.7 6.2 all-gather.12.cloned.1.call-done
  344.8 3.0 fusion.15
  348.6 85.9 %all-reduce.20.cloned.1.call-done = f32[1,64,1024]{2,1,0:T(8,128)} async-done(((f32[1,64,1024]{2,1,0:T(8,128)}), f32[1,64,1024]{2,1,0:T(8,128)}) %all-reduce.20.cloned.1.call-update) | async-done | bytes 262160 | tf_op jit(solution)/shard_map/psum | solution.py:33
  434.5 1.1 bitcast_subtract_fusion.2
  435.5 2.2 all_gather.37
  437.7 2.4 convolution_bitcast_fusion.5
  440.3 84.4 %all-reduce.22.cloned.1.call-done = f32[1,64,1024]{2,1,0:T(8,128)} async-done(((f32[1,64,1024]{2,1,0:T(8,128)}), f32[1,64,1024]{2,1,0:T(8,128)}) %all-reduce.22.cloned.1.call-update) | async-done | bytes 262160 | tf_op jit(solution)/shard_map/psum | solution.py:36
  524.7 2.6 all_gather.38
  527.2 6.1 fusion
  533.7 4.9 convolution_bitcast_fusion
  538.7 4.7 reshape.130
  545.4 151.0 %all-reduce.24.cloned.1.call-done = f32[2,7,64,1024]{3,2,0,1:T(8,128)} async-done(((f32[2,7,64,1024]{3,2,0,1:T(8,128)}), f32[2,7,64,1024]{3,2,0,1:T(8,128)}) %all-reduce.24.cloned.1.call-update) | async-done | bytes 3670032 | tf_op jit(solution)/shard_map/psum | solution.py:72
  696.4 2.4 bitcast_subtract_fusion
  698.8 2.2 all_gather.39
  701.0 2.4 convolution_bitcast_fusion.4
  703.5 1.3 fusion.69
  707.2 79.6 %all-reduce.26.cloned.1.call-done = f32[1,64,1024]{2,1,0:T(8,128)} async-done(((f32[1,64,1024]{2,1,0:T(8,128)}), f32[1,64,1024]{2,1,0:T(8,128)}) %all-reduce.26.cloned.1.call-update) | async-done | bytes 262160 | tf_op jit(solution)/shard_map/psum | solution.py:36
  786.8 2.5 all_gather.40
  789.4 2.5 convolution_bitcast_fusion.1
  793.5 1.2 multiply_multiply_fusion
  794.7 53.8 %all-reduce.36.cloned.1.call-done = (f32[1,64,1024]{2,1,0:T(8,128)}, f32[2,64,1024]{2,1,0:T(8,128)}, f32[4,64,1024]{2,1,0:T(8,128)}) async-done(((f32[1,64,1024]{2,1,0:T(8,128)}, f32[2,64,1024]{2,1,0:T(8,128)}, f32[4,64,1024]{2,1,0:T(8,128)}), (f32[1,64,1024]{2,1,0:T(8,128)}, f32[2,64,1024]{2,1,0:T(8,128)}, f32[4,64,1024]{2,1,0:T(8,128)})) %all-reduce.36.cloned.1.call-update) | async-done | bytes 1835024 | tf_op jit(solution)/shard_map/psum | solution.py:89
  848.6 88.8 %all-reduce.28.cloned.1.call-done = f32[2,64,1024]{2,1,0:T(8,128)} async-done(((f32[2,64,1024]{2,1,0:T(8,128)}), f32[2,64,1024]{2,1,0:T(8,128)}) %all-reduce.28.cloned.1.call-update) | async-done | bytes 524304 | tf_op jit(solution)/shard_map/psum | solution.py:33
  937.4 1.9 slice_subtract_fusion
  939.4 11.1 all-gather.14.cloned.1.call-done
  950.6 3.3 fusion.21
  953.9 87.4 %all-reduce.30.cloned.1.call-done = f32[2,64,1024]{2,1,0:T(8,128)} async-done(((f32[2,64,1024]{2,1,0:T(8,128)}), f32[2,64,1024]{2,1,0:T(8,128)}) %all-reduce.30.cloned.1.call-update) | async-done | bytes 524304 | tf_op jit(solution)/shard_map/psum | solution.py:36
  1041.4 12.5 %all-gather.16.cloned.1.call-done = f32[2,64,2048]{2,1,0:T(8,128)} async-done(((f32[2,64,1024]{2,1,0:T(8,128)}), f32[2,64,2048]{2,1,0:T(8,128)}) %all-gather.16.cloned.1.call-update) | async-done | bytes 1048592 | tf_op jit(solution)/shard_map/all_gather | solution.py:37
  1053.9 3.2 fusion.16
  1057.2 86.8 %all-reduce.32.cloned.1.call-done = f32[1,64,1024]{2,1,0:T(8,128)} async-done(((f32[1,64,1024]{2,1,0:T(8,128)}), f32[1,64,1024]{2,1,0:T(8,128)}) %all-reduce.32.cloned.1.call-update) | async-done | bytes 262160 | tf_op jit(solution)/shard_map/psum | solution.py:33
  1144.0 1.0 slice_subtract_fusion.1
  1145.0 2.2 all_gather.43
  1147.2 2.4 convolution_bitcast_fusion.2
  1149.6 2.4 maximum_bitcast_fusion
  1152.1 82.0 %all-reduce.34.cloned.1.call-done = f32[1,64,1024]{2,1,0:T(8,128)} async-done(((f32[1,64,1024]{2,1,0:T(8,128)}), f32[1,64,1024]{2,1,0:T(8,128)}) %all-reduce.34.cloned.1.call-update) | async-done | bytes 262160 | tf_op jit(solution)/shard_map/psum | solution.py:36
  1234.1 2.3 pad_maximum_fusion
  (69 shorter events, 7.7 us)
Async XLA Ops:
  7.2 326.8 %copy-start = (s32[1,7,16]{2,0,1:T(1,128)S(1)}, s32[1,7,16]{2,0,1:T(1,128)}, u32[]{:S(2)}) copy-start(s32[1,7,16]{2,0,1:T(1,128)} %param.14) | copy-start | bytes 1348
  7.2 18.8 %all-gather.18.cloned.1.call-start = ((), (), s32[]{:S(2)}) async-start(), calls=%async_computation.16 | async-start | bytes 3145728 | tf_op jit(solution)/shard_map/all_gather | solution.py:34
  9.6 110.4 %all-reduce.14.cloned.1.call-start = ((), (), s32[]{:S(2)}) async-start(), calls=%async_computation | async-start | bytes 2097152 | tf_op jit(solution)/shard_map/psum | solution.py:36
  31.0 103.1 %all-gather.8.cloned.1.call-start = ((), (), s32[]{:S(2)}) async-start(), calls=%async_computation.1 | async-start | bytes 3145728 | tf_op jit(solution)/shard_map/all_gather | solution.py:37
  120.0 107.2 %all-reduce.16.cloned.1.call-start = ((), (), s32[]{:S(2)}) async-start(), calls=%async_computation.2 | async-start | bytes 1048576 | tf_op jit(solution)/shard_map/psum | solution.py:33
  139.9 191.4 %copy-start.7 = (s32[4]{0:T(128)S(1)}, s32[4]{0:T(128)}, u32[]{:S(2)}) copy-start(s32[4]{0:T(128)} %param.18) | copy-start | bytes 52
  139.9 192.0 %copy-start.8 = (s32[4]{0:T(128)S(1)}, s32[4]{0:T(128)}, u32[]{:S(2)}) copy-start(s32[4]{0:T(128)} %param.19) | copy-start | bytes 52
  139.9 100.5 %all-gather.10.cloned.1.call-start = ((), (), s32[]{:S(2)}) async-start(), calls=%async_computation.3 | async-start | bytes 1572864 | tf_op jit(solution)/shard_map/all_gather | solution.py:34
  229.3 102.0 %all-reduce.18.cloned.1.call-start = ((), (), s32[]{:S(2)}) async-start(), calls=%async_computation.4 | async-start | bytes 1048576 | tf_op jit(solution)/shard_map/psum | solution.py:36
  243.8 100.2 %all-gather.12.cloned.1.call-start = ((), (), s32[]{:S(2)}) async-start(), calls=%async_computation.5 | async-start | bytes 1572864 | tf_op jit(solution)/shard_map/all_gather | solution.py:37
  331.3 103.2 %all-reduce.20.cloned.1.call-start = ((), (), s32[]{:S(2)}) async-start(), calls=%async_computation.6 | async-start | bytes 524288 | tf_op jit(solution)/shard_map/psum | solution.py:33
  347.9 176.8 %all-reduce.22.cloned.1.call-start = ((), (), s32[]{:S(2)}) async-start(), calls=%async_computation.7 | async-start | bytes 524288 | tf_op jit(solution)/shard_map/psum | solution.py:36
  440.1 256.2 %all-reduce.24.cloned.1.call-start = ((), (), s32[]{:S(2)}) async-start(), calls=%async_computation.8 | async-start | bytes 7340032 | tf_op jit(solution)/shard_map/psum | solution.py:72
  543.4 243.4 %all-reduce.26.cloned.1.call-start = ((), (), s32[]{:S(2)}) async-start(), calls=%async_computation.9 | async-start | bytes 524288 | tf_op jit(solution)/shard_map/psum | solution.py:36
  703.4 145.1 %all-reduce.36.cloned.1.call-start = ((), (), s32[]{:S(2)}) async-start(), calls=%async_computation.17 | async-start | bytes 3670016 | tf_op jit(solution)/shard_map/psum | solution.py:89
  786.8 6.7 copy-start.6
  794.7 142.7 %all-reduce.28.cloned.1.call-start = ((), (), s32[]{:S(2)}) async-start(), calls=%async_computation.10 | async-start | bytes 1048576 | tf_op jit(solution)/shard_map/psum | solution.py:33
  848.5 102.0 %all-gather.14.cloned.1.call-start = ((), (), s32[]{:S(2)}) async-start(), calls=%async_computation.11 | async-start | bytes 1572864 | tf_op jit(solution)/shard_map/all_gather | solution.py:34
  939.4 102.0 %all-reduce.30.cloned.1.call-start = ((), (), s32[]{:S(2)}) async-start(), calls=%async_computation.12 | async-start | bytes 1048576 | tf_op jit(solution)/shard_map/psum | solution.py:36
  953.9 100.0 %all-gather.16.cloned.1.call-start = ((), (), s32[]{:S(2)}) async-start(), calls=%async_computation.13 | async-start | bytes 1572864 | tf_op jit(solution)/shard_map/all_gather | solution.py:37
  1041.4 102.6 %all-reduce.32.cloned.1.call-start = ((), (), s32[]{:S(2)}) async-start(), calls=%async_computation.14 | async-start | bytes 524288 | tf_op jit(solution)/shard_map/psum | solution.py:33
  1053.9 95.7 %copy-start.2 = (f32[4,64,1024]{2,1,0:T(8,128)S(1)}, f32[4,64,1024]{2,1,0:T(8,128)}, u32[]{:S(2)}) copy-start(f32[4,64,1024]{2,1,0:T(8,128)} %all-reduce.14.cloned.1.call-done) | copy-start | bytes 3145732
  1053.9 95.7 %copy-start.3 = (f32[2,64,1024]{2,1,0:T(8,128)S(1)}, f32[2,64,1024]{2,1,0:T(8,128)}, u32[]{:S(2)}) copy-start(f32[2,64,1024]{2,1,0:T(8,128)} %all-reduce.18.cloned.1.call-done) | copy-start | bytes 1572868
  1057.2 177.0 %all-reduce.34.cloned.1.call-start = ((), (), s32[]{:S(2)}) async-start(), calls=%async_computation.15 | async-start | bytes 524288 | tf_op jit(solution)/shard_map/psum | solution.py:36
  1149.6 84.6 %copy-start.4 = (f32[2,64,1024]{2,1,0:T(8,128)S(1)}, f32[2,64,1024]{2,1,0:T(8,128)}, u32[]{:S(2)}) copy-start(f32[2,64,1024]{2,1,0:T(8,128)} %all-reduce.30.cloned.1.call-done) | copy-start | bytes 1572868
  1149.6 84.6 %copy-start.5 = (f32[4,64,1024]{2,1,0:T(8,128)S(1)}, f32[4,64,1024]{2,1,0:T(8,128)}, u32[]{:S(2)}) copy-start(f32[4,64,1024]{2,1,0:T(8,128)} %get-tuple-element.4) | copy-start | bytes 3145732
  1149.6 86.9 %copy-start.1 = (s32[1,7,16]{2,0,1:T(1,128)S(1)}, s32[1,7,16]{2,0,1:T(1,128)}, u32[]{:S(2)}) copy-start(s32[1,7,16]{2,0,1:T(1,128)} %param.14) | copy-start | bytes 1348
Sparse Core Ops, SparseCore 0:
  10.2 15.7 all-gather.17
  31.2 88.7 all-reduce.13
  121.7 12.4 all-gather.7
  140.0 87.0 all-reduce.15
  229.4 11.0 all-gather.9
  244.1 87.1 all-reduce.17
  332.9 11.0 all-gather.11
  348.0 86.4 all-reduce.19
  440.3 84.3 all-reduce.21
  543.5 152.8 all-reduce.23
  703.5 83.2 all-reduce.25
  794.8 53.6 all-reduce.35
  851.7 85.6 all-reduce.27
  939.5 11.0 all-gather.13
  954.2 87.1 all-reduce.29
  1042.9 11.0 all-gather.15
  1057.5 86.4 all-reduce.31
  1149.7 84.3 all-reduce.33
where the time goes:
time: 1240 us
  waiting for transfers between devices  1130 us (91%)
  matrix products  47.1 us (4%)
  other arithmetic  21.3 us (2%)
  between operations  18.2 us (1%)
    psum x6, waiting for transfers between devices, solve_level(): x_rows = lax.psum(x_part, 'col')  510 us
    psum x4, waiting for transfers between devices, solve_level(): y_rows = known - lax.psum(partial_value, 'col')  349 us
    psum x1, waiting for transfers between devices, per_device(): total_update = lax.psum(spread, ('leaf', 'row', 'col'))  151 us
    psum x1, waiting for transfers between devices, per_device(): lax.psum((sol_term, mid_term, root_term), 'leaf')  53.8 us
    dot_general x11, matrix products, apply_block(): jnp.einsum('btc,brc->btr', vectors, matrices, precision=lax.Precision.HIG...  39.7 us
    all_gather x3, waiting for transfers between devices, solve_level(): y_full = lax.all_gather(y_rows, 'row', axis=2, tiled=True)  38.6 us
    all_gather x3, waiting for transfers between devices, solve_level(): x_full = lax.all_gather(x_rows, 'row', axis=2, tiled=True)  32.8 us
  transfers between devices with their start and end apart: 18, of which 18 were waited for; matrix products, arithmetic and copies ran while one was open for 1% of the time, Pallas kernels for 0%

commit v1 on v0

v1 whole, which is shorter than its diff:
```python
import jax
import jax.numpy as jnp
from jax import lax
from jax.sharding import PartitionSpec as P

BLOCK = 128


def apply_block(vectors, matrices):
    return jnp.einsum("btc,brc->btr", vectors, matrices, precision=lax.Precision.HIGHEST)


def per_device(
    sec_rhs, sec_inv, sec_low, sec_top, sec_rows, top_rhs, top_inv, top_low, sec_parent, top_parent
):
    here_row = lax.axis_index("row")
    here_col = lax.axis_index("col")
    here_leaf = lax.axis_index("leaf")
    parts_col = lax.axis_size("col")
    parts_leaf = lax.axis_size("leaf")
    rows_here = sec_rhs.shape[-1]
    cols_here = sec_inv.shape[-1]
    per_half = rows_here // cols_here
    nrhs = sec_rhs.shape[2]
    swap = [(0, 1), (1, 0)]

    def to_cols(known):
        at = jnp.clip(here_col - per_half * here_row, 0, per_half - 1)
        mine = lax.dynamic_slice_in_dim(known, at * cols_here, cols_here, 2)
        other = lax.ppermute(mine, "row", swap)
        return jnp.where(here_col // per_half == here_row, mine, other)

    def reduce_to_cols(partial):
        n = partial.shape[0]
        other = lax.ppermute(partial, "row", swap)
        low = jnp.where(here_row == 0, partial, other)
        high = jnp.where(here_row == 0, other, partial)
        full = jnp.concatenate([low, high], axis=2)
        chunks = full.reshape(n, nrhs, parts_col, cols_here).transpose(2, 0, 1, 3)
        got = lax.all_to_all(chunks, "col", 0, 0, tiled=True)
        return got.sum(0)

    def cols_to_rows(cols):
        m = cols.shape[0]
        got = lax.all_gather(cols, "col", axis=0, tiled=False)
        half = lax.dynamic_slice_in_dim(got, here_row * per_half, per_half, 0)
        return half.transpose(1, 2, 0, 3).reshape(m, nrhs, rows_here)

    rhs_cols = to_cols(sec_rhs[0])
    top_rhs_cols = to_cols(top_rhs)
    inverse = sec_inv[0]
    lower = sec_low[0]

    x_leaf = reduce_to_cols(apply_block(rhs_cols[0:4], inverse[0:4]))
    acc_mid = apply_block(x_leaf, lower[0:4]).reshape(2, 2, nrhs, rows_here).sum(1)
    acc_root = apply_block(x_leaf, lower[4:8]).sum(0, keepdims=True)
    y_mid = rhs_cols[4:6] - reduce_to_cols(acc_mid)
    x_mid = reduce_to_cols(apply_block(y_mid, inverse[4:6]))
    acc_root = acc_root + apply_block(x_mid, lower[8:10]).sum(0, keepdims=True)
    y_root = rhs_cols[6:7] - reduce_to_cols(acc_root)
    x_root = reduce_to_cols(apply_block(y_root, inverse[6:7]))
    sec_cols = jnp.concatenate([x_leaf, x_mid, x_root], axis=0)
    sec_out = cols_to_rows(sec_cols)[None]

    block_rows = sec_top.shape[2] // BLOCK
    nblk = rows_here * 2 // BLOCK
    contrib = apply_block(sec_cols, sec_top[0]).reshape(7, nrhs, block_rows, BLOCK)
    mine = lax.dynamic_slice_in_dim(sec_rows[0], here_row * block_rows, block_rows, 1)
    path_ids = jnp.arange(3 * nblk, dtype=jnp.int32)
    one_hot = (mine[:, :, None] == path_ids[None, None, :]).astype(jnp.float32)
    placed = jnp.einsum("ntkl,nkb->btl", contrib, one_hot, precision=lax.Precision.HIGHEST)
    section_ids = jnp.arange(sec_parent.shape[0], dtype=jnp.int32)
    parent_node = jnp.sum(jnp.where(section_ids == here_leaf, sec_parent, 0))
    grand_node = jnp.sum(jnp.where(jnp.arange(4, dtype=jnp.int32) == parent_node, top_parent, 0))
    mid_part = placed[nblk : 2 * nblk]
    zeros = jnp.zeros_like(mid_part)
    spread = jnp.stack(
        [
            placed[0:nblk],
            jnp.where(grand_node == 0, mid_part, zeros),
            jnp.where(grand_node == 1, mid_part, zeros),
            placed[2 * nblk : 3 * nblk],
        ]
    )
    spread = spread + lax.ppermute(spread, "row", swap)
    gathered = lax.all_to_all(spread.transpose(1, 0, 2, 3), "col", 0, 0, tiled=True).sum(0)

    rhs_own = lax.dynamic_index_in_dim(top_rhs_cols, parent_node, 0, keepdims=True)
    inverse_own = lax.dynamic_slice_in_dim(top_inv, parent_node, 1, 0)
    y_three = rhs_own - gathered[0:1]
    x_three = reduce_to_cols(apply_block(y_three, inverse_own))
    payload = jnp.concatenate([x_three, gathered[1:4]], axis=0)
    fanned = jnp.broadcast_to(payload[None], (parts_leaf,) + payload.shape)
    by_leaf = lax.all_to_all(fanned, "leaf", 0, 0, tiled=True)
    upper_update = by_leaf[:, 1:4].sum(0)
    which = sec_parent[None, :] == jnp.arange(4, dtype=jnp.int32)[:, None]
    x_by_leaf = by_leaf[:, 0]
    sol_three = jnp.sum(jnp.where(which[:, :, None, None], x_by_leaf[None], 0.0), axis=1)

    to_mid = apply_block(sol_three, top_low[0:8:2])
    parent_hot = top_parent[:, None] == jnp.arange(2, dtype=jnp.int32)[None, :]
    acc_four = jnp.sum(jnp.where(parent_hot.T[:, :, None, None], to_mid[None], 0.0), axis=1)
    acc_top = apply_block(sol_three, top_low[1:8:2]).sum(0, keepdims=True)
    y_four = top_rhs_cols[4:6] - upper_update[0:2] - reduce_to_cols(acc_four)
    x_four = reduce_to_cols(apply_block(y_four, top_inv[4:6]))
    rows_early = cols_to_rows(jnp.concatenate([sol_three, x_four], axis=0))
    acc_top = acc_top + apply_block(x_four, top_low[8:10]).sum(0, keepdims=True)
    y_five = top_rhs_cols[6:7] - upper_update[2:3] - reduce_to_cols(acc_top)
    x_five = reduce_to_cols(apply_block(y_five, top_inv[6:7]))
    top_out = jnp.concatenate([rows_early, cols_to_rows(x_five)], axis=0)
    return (sec_out, top_out)


def solution(mesh):
    placed = (
        P("leaf", None, None, "row"),
        P("leaf", None, "row", "col"),
        P("leaf", None, "row", "col"),
        P("leaf", None, "row", "col"),
        P("leaf", None, None),
        P(None, None, "row"),
        P(None, "row", "col"),
        P(None, "row", "col"),
        P(),
        P(),
    )
    return jax.shard_map(
        per_device,
        mesh=mesh,
        in_specs=placed,
        out_specs=(P("leaf", None, None, "row"), P(None, None, "row")),
        check_vma=False,
    )
```

time: 1240 us -> 378 us (0.30)
  waiting for transfers between devices: 1130 us -> 134 us
  blocking collectives: 11.6 us -> 130 us
  starting transfers between devices: 0.73 us -> 27.9 us
    psum x12 -> x0, waiting for transfers between devices: 1060 us -> none  [the longest x6 510 us: solve_level(): x_rows = lax.psum(x_part, 'col')]
    all_to_all x0 -> x7, waiting for transfers between devices: none -> 110 us  [the longest x5 71.7 us: reduce_to_cols(): got = lax.all_to_all(chunks, 'col', 0, 0, tiled=True)]
    all_to_all x0 -> x5, blocking collectives: none -> 108 us  [reduce_to_cols(): got = lax.all_to_all(chunks, 'col', 0, 0, tiled=True)]
    all_gather x6 -> x2, waiting for transfers between devices: 71.5 us -> 0.04 us  [cols_to_rows(): got = lax.all_gather(cols, 'col', axis=0, tiled=False)]
    all_to_all x0 -> x7, starting transfers between devices: none -> 26.3 us  [the longest x5 18.2 us: reduce_to_cols(): got = lax.all_to_all(chunks, 'col', 0, 0, tiled=True)]
    ppermute x0 -> x13, waiting for transfers between devices: none -> 23.3 us  [the longest x10 17.7 us: reduce_to_cols(): other = lax.ppermute(partial, 'row', swap)]
    dot_general x11 -> x13, matrix products: 39.7 us -> 40.2 us  [apply_block(): jnp.einsum('btc,brc->btr', vectors, matrices, precision=lax.Precision.HIG...]
  transfers between devices with their start and end apart: 18 -> 22, of which waited for: 18 -> 19; matrix products, arithmetic and copies ran while one was open for 1% -> 9% of each run, Pallas kernels for 0% -> 0%
where the time goes in v1:
time: 378 us; the launch traced here: 376 us
  waiting for transfers between devices  134 us (35%)
  blocking collectives  130 us (34%)
  matrix products  41.2 us (11%)
  starting transfers between devices  27.9 us (7%)
  between operations  17.9 us (5%)
  other arithmetic  14.5 us (4%)
  local copies, waits for them, and re-layouts  11.4 us (3%)
    all_to_all x5, blocking collectives, reduce_to_cols(): got = lax.all_to_all(chunks, 'col', 0, 0, tiled=True)  108 us
    all_to_all x5, waiting for transfers between devices, reduce_to_cols(): got = lax.all_to_all(chunks, 'col', 0, 0, tiled=True)  71.7 us
    dot_general x13, matrix products, apply_block(): jnp.einsum('btc,brc->btr', vectors, matrices, precision=lax.Precision.HIG...  40.2 us
    all_to_all x1, waiting for transfers between devices, per_device(): lax.all_to_all(spread.transpose(1, 0, 2, 3), 'col', 0, 0, tiled=True).sum(0)  30.4 us
    all_gather x1, blocking collectives, cols_to_rows(): got = lax.all_gather(cols, 'col', axis=0, tiled=False)  21.8 us
    all_to_all x5, starting transfers between devices, reduce_to_cols(): got = lax.all_to_all(chunks, 'col', 0, 0, tiled=True)  18.2 us
    ppermute x10, waiting for transfers between devices, reduce_to_cols(): other = lax.ppermute(partial, 'row', swap)  17.7 us
    all_to_all x1, waiting for transfers between devices, per_device(): by_leaf = lax.all_to_all(fanned, 'leaf', 0, 0, tiled=True)  8.07 us
  transfers between devices with their start and end apart: 22, of which 19 were waited for; matrix products, arithmetic and copies ran while one was open for 9% of the time, Pallas kernels for 0%

profile of v1, /device:TPU:0, one launch (start us, length us, event | category | flops | bytes accessed | tf_op | source)
XLA Modules:
  0.0 376.1 jit_solution(17149731024537687206)
XLA Ops:
  10.7 3.9 %fusion.6 = f32[4,64,1024]{2,1,0:T(8,128)S(1)} fusion(f32[7,64,128]{2,1,0:T(8,128)S(1)} %broadcast_select_fusion.21, f32[1,7,1024,128]{3,2,1,0:T(8,128)} %param.11), kind=kOutput, calls=%fused_computation.9 | convolution fusion | flops 402653184 | bytes 3375104 | tf_op jit(solution)/shard_map/btc,brc->btr/dot_general | solution.py:10
  14.9 2.5 collective-permute-done.1
  17.8 36.7 %all_to_all.60 = f32[16,4,64,128]{3,2,1,0:T(8,128)S(1)} all-to-all(f32[16,4,64,128]{3,2,1,0:T(8,128)S(1)} %bitcast_bitcast_fusion), channel_id=1, replica_groups=mesh['leaf'=4,'row'=2,'col'=16] {'col'}, dimensions={0} | all-to-all | bytes 4194304 | tf_op jit(solution)/shard_map/all_to_all | solution.py:40
  54.6 4.0 %bitcast_reduce_fusion = f32[2,64,1024]{2,1,0:T(8,128)S(1)} fusion(f32[4,64,128]{2,1,0:T(8,128)S(1)} %reduce_sum.177, f32[1,10,1024,128]{3,2,1,0:T(8,128)} %param.12), kind=kOutput, calls=%fused_computation.49 | convolution fusion | flops 402784256 | bytes 2752512 | tf_op jit(solution)/shard_map/btc,brc->btr/dot_general | solution.py:10
  58.7 1.9 collective-permute-done.2
  60.8 20.4 %all_to_all.61 = f32[16,2,64,128]{3,2,1,0:T(8,128)S(1)} all-to-all(f32[16,2,64,128]{3,2,1,0:T(8,128)S(1)} %bitcast_bitcast_fusion.4), channel_id=1, replica_groups=mesh['leaf'=4,'row'=2,'col'=16] {'col'}, dimensions={0} | all-to-all | bytes 2097152 | tf_op jit(solution)/shard_map/all_to_all | solution.py:40
  81.3 2.5 fusion.31
  83.8 1.9 collective-permute-done.3
  86.9 3.7 all-to-all-start.2
  90.6 3.7 fusion.25
  94.3 14.6 %all-to-all-done.2 = f32[16,2,64,128]{3,2,1,0:T(8,128)S(1)} async-done(((f32[16,2,64,128]{3,2,1,0:T(8,128)}), f32[16,2,64,128]{3,2,1,0:T(8,128)S(1)}, u32[]{:S(2)}, u32[]{:S(2)}) %all-to-all-start.2) | async-done | bytes 1048608 | tf_op jit(solution)/shard_map/all_to_all | solution.py:40
  109.0 2.3 fusion.29
  111.4 1.5 collective-permute-done.4
  113.0 14.8 %all_to_all.62 = f32[16,1,64,128]{3,2,1,0:T(8,128)S(1)} all-to-all(f32[16,1,64,128]{3,2,1,0:T(8,128)S(1)} %bitcast_bitcast_fusion.9), channel_id=1, replica_groups=mesh['leaf'=4,'row'=2,'col'=16] {'col'}, dimensions={0} | all-to-all | bytes 1048576 | tf_op jit(solution)/shard_map/all_to_all | solution.py:40
  127.8 1.7 convolution_bitcast_fusion.3
  129.7 1.5 collective-permute-done.5
  132.1 3.8 all-to-all-start.4
  139.3 8.4 %all-to-all-done.4 = f32[16,1,64,128]{3,2,1,0:T(8,128)S(1)} async-done(((f32[16,1,64,128]{3,2,1,0:T(8,128)}), f32[16,1,64,128]{3,2,1,0:T(8,128)S(1)}, u32[]{:S(2)}, u32[]{:S(2)}) %all-to-all-start.4) | async-done | bytes 524320 | tf_op jit(solution)/shard_map/all_to_all | solution.py:40
  147.8 6.1 %fusion = f32[7,64,1024]{2,1,0:T(8,128)S(1)} fusion(f32[1,7,1024,128]{3,2,1,0:T(8,128)} %param.13, f32[1,64,128]{2,1,0:T(8,128)S(1)} %bitcast.218, f32[2,64,128]{2,1,0:T(8,128)S(1)} %reduce_sum.180, f32[4,64,128]{2,1,0:T(8,128)S(1)} %reduce_sum.177), kind=kOutput, calls=%fused_computation | convolution fusion | flops 704757760 | bytes 5734400 | tf_op jit(solution)/shard_map/btc,brc->btr/dot_general | solution.py:10
  155.7 4.1 %collective-permute-done.7 = f32[4,16,64,128]{3,1,2,0:T(8,128)S(1)} collective-permute-done((f32[4,16,64,128]{3,1,2,0:T(8,128)S(1)}, f32[4,16,64,128]{3,1,2,0:T(8,128)S(1)}, u32[]{:S(2)}, u32[]{:S(2)}) %collective-permute-start.7) | collective-permute-done | bytes 2097184 | tf_op jit(solution)/shard_map/ppermute | solution.py:85
  160.1 2.0 copy.51
  162.1 3.7 all-to-all-start.5
  170.7 30.4 %all-to-all-done.5 = f32[16,4,64,128]{3,2,1,0:T(8,128)S(1)} async-done(((f32[16,4,64,128]{3,2,1,0:T(8,128)}), f32[16,4,64,128]{3,2,1,0:T(8,128)S(1)}, u32[]{:S(2)}, u32[]{:S(2)}) %all-to-all-start.5) | async-done | bytes 2097184 | tf_op jit(solution)/shard_map/all_to_all | solution.py:86
  201.2 1.7 convolution_bitcast_fusion.2
  203.1 1.5 collective-permute-done.8
  205.5 3.6 all-to-all-start.6
  209.1 16.5 %all-to-all-done.6 = f32[16,1,64,128]{3,2,1,0:T(8,128)S(1)} async-done(((f32[16,1,64,128]{3,2,1,0:T(8,128)}), f32[16,1,64,128]{3,2,1,0:T(8,128)S(1)}, u32[]{:S(2)}, u32[]{:S(2)}) %all-to-all-start.6) | async-done | bytes 524320 | tf_op jit(solution)/shard_map/all_to_all | solution.py:40
  226.5 4.3 %all-to-all-start.7 = ((f32[4,4,64,128]{3,2,1,0:T(8,128)}), f32[4,4,64,128]{3,2,1,0:T(8,128)S(1)}, u32[]{:S(2)}, u32[]{:S(2)}) async-start(f32[4,4,64,128]{3,2,1,0:T(8,128)} %broadcast_in_dim.72), calls=%async_computation.7 | async-start | bytes 1048576 | tf_op jit(solution)/shard_map/all_to_all | solution.py:94
  230.9 8.1 %all-to-all-done.7 = f32[4,4,64,128]{3,2,1,0:T(8,128)S(1)} async-done(((f32[4,4,64,128]{3,2,1,0:T(8,128)}), f32[4,4,64,128]{3,2,1,0:T(8,128)S(1)}, u32[]{:S(2)}, u32[]{:S(2)}) %all-to-all-start.7) | async-done | bytes 524320 | tf_op jit(solution)/shard_map/all_to_all | solution.py:94
  239.0 4.0 %fusion.10 = f32[4,64,1024]{2,1,0:T(8,128)S(1)} fusion(f32[4,64,128]{2,1,0:T(8,128)S(1)} %select_reduce_fusion.1, f32[10,1024,128]{2,1,0:T(8,128)} %param.17), kind=kOutput, calls=%fused_computation.14 | convolution fusion | flops 402653184 | bytes 3276800 | tf_op jit(solution)/shard_map/btc,brc->btr/dot_general | solution.py:10
  243.3 1.9 collective-permute-done.9
  246.5 3.7 all-to-all-start.8
  250.2 18.2 %all-to-all-done.8 = f32[16,2,64,128]{3,2,1,0:T(8,128)S(1)} async-done(((f32[16,2,64,128]{3,2,1,0:T(8,128)}), f32[16,2,64,128]{3,2,1,0:T(8,128)S(1)}, u32[]{:S(2)}, u32[]{:S(2)}) %all-to-all-start.8) | async-done | bytes 1048608 | tf_op jit(solution)/shard_map/all_to_all | solution.py:40
  268.5 2.5 fusion.34
  271.3 1.9 collective-permute-done.10
  273.4 20.4 %all_to_all.63 = f32[16,2,64,128]{3,2,1,0:T(8,128)S(1)} all-to-all(f32[16,2,64,128]{3,2,1,0:T(8,128)S(1)} %bitcast_bitcast_fusion.1), channel_id=1, replica_groups=mesh['leaf'=4,'row'=2,'col'=16] {'col'}, dimensions={0} | all-to-all | bytes 2097152 | tf_op jit(solution)/shard_map/all_to_all | solution.py:40
  294.6 3.7 fusion.22
  298.3 2.3 fusion.28
  300.7 1.5 collective-permute-done.11
  302.4 15.7 %all_to_all.64 = f32[16,1,64,128]{3,2,1,0:T(8,128)S(1)} all-to-all(f32[16,1,64,128]{3,2,1,0:T(8,128)S(1)} %bitcast_bitcast_fusion.6), channel_id=1, replica_groups=mesh['leaf'=4,'row'=2,'col'=16] {'col'}, dimensions={0} | all-to-all | bytes 1048576 | tf_op jit(solution)/shard_map/all_to_all | solution.py:40
  318.1 1.7 convolution_bitcast_fusion
  319.9 1.5 collective-permute-done.12
  322.3 3.6 all-to-all-start.11
  325.9 1.7 dynamic-slice_bitcast_fusion
  328.7 1.5 broadcast_in_dim_reshape.3
  330.2 14.0 %all-to-all-done.11 = f32[16,1,64,128]{3,2,1,0:T(8,128)S(1)} async-done(((f32[16,1,64,128]{3,2,1,0:T(8,128)}), f32[16,1,64,128]{3,2,1,0:T(8,128)S(1)}, u32[]{:S(2)}, u32[]{:S(2)}) %all-to-all-start.11) | async-done | bytes 524320 | tf_op jit(solution)/shard_map/all_to_all | solution.py:40
  344.2 21.8 %all-gather.2 = f32[1024,128]{1,0:T(8,128)S(1)} all-gather(f32[64,128]{1,0:T(8,128)S(1)} %reduce_sum.197), channel_id=4, replica_groups=mesh['leaf'=4,'row'=2,'col'=16] {'col'}, dimensions={0}, use_global_device_ids=true | all-gather | bytes 557056 | tf_op jit(solution)/shard_map/all_gather | solution.py:45
  366.3 1.6 copy_bitcast_fusion
  (89 shorter events, 23.2 us)
Async XLA Ops:
  7.2 132.1 %copy-start = (s32[1,7,16]{2,0,1:T(1,128)S(1)}, s32[1,7,16]{2,0,1:T(1,128)}, u32[]{:S(2)}) copy-start(s32[1,7,16]{2,0,1:T(1,128)} %param.14) | copy-start | bytes 1348
  8.2 1.6 collective-permute-start
  14.7 2.7 collective-permute-start.1
  58.6 2.0 collective-permute-start.2
  83.7 2.0 collective-permute-start.3
  86.9 22.0 %all-to-all-start.2 = ((f32[16,2,64,128]{3,2,1,0:T(8,128)}), f32[16,2,64,128]{3,2,1,0:T(8,128)S(1)}, u32[]{:S(2)}, u32[]{:S(2)}) async-start(f32[16,2,64,128]{3,2,1,0:T(8,128)} %bitcast_bitcast_fusion.3), calls=%async_computation.2 | async-start | bytes 2097152 | tf_op jit(solution)/shard_map/all_to_all | solution.py:40
  111.3 1.6 collective-permute-start.4
  127.8 8.0 %copy-start.2 = (s32[4]{0:T(128)S(1)}, s32[4]{0:T(128)}, u32[]{:S(2)}) copy-start(s32[4]{0:T(128)} %param.18) | copy-start | bytes 52
  127.8 8.7 %copy-start.3 = (s32[4]{0:T(128)S(1)}, s32[4]{0:T(128)}, u32[]{:S(2)}) copy-start(s32[4]{0:T(128)} %param.19) | copy-start | bytes 52
  129.6 1.6 collective-permute-start.5
  132.1 15.7 %all-to-all-start.4 = ((f32[16,1,64,128]{3,2,1,0:T(8,128)}), f32[16,1,64,128]{3,2,1,0:T(8,128)S(1)}, u32[]{:S(2)}, u32[]{:S(2)}) async-start(f32[16,1,64,128]{3,2,1,0:T(8,128)} %bitcast_bitcast_fusion.8), calls=%async_computation.4 | async-start | bytes 1048576 | tf_op jit(solution)/shard_map/all_to_all | solution.py:40
  155.6 4.2 %collective-permute-start.7 = (f32[4,16,64,128]{3,1,2,0:T(8,128)S(1)}, f32[4,16,64,128]{3,1,2,0:T(8,128)S(1)}, u32[]{:S(2)}, u32[]{:S(2)}) collective-permute-start(f32[4,16,64,128]{3,1,2,0:T(8,128)S(1)} %pad_maximum_fusion), channel_id=1, source_target_pairs={{0,16},{16,0},{1,17},{17,1},{2,18},{18,2},{3,19},{19,3},{4,20},{20... | collective-permute-start | bytes 6291464 | tf_op jit(solution)/shard_map/ppermute | solution.py:85
  162.1 39.0 %all-to-all-start.5 = ((f32[16,4,64,128]{3,2,1,0:T(8,128)}), f32[16,4,64,128]{3,2,1,0:T(8,128)S(1)}, u32[]{:S(2)}, u32[]{:S(2)}) async-start(f32[16,4,64,128]{3,2,1,0:T(8,128)} %copy.51), calls=%async_computation.5 | async-start | bytes 4194304 | tf_op jit(solution)/shard_map/all_to_all | solution.py:86
  165.8 160.1 %all-gather.6.cloned.1.call-start = ((), (), s32[]{:S(2)}) async-start(), calls=%async_computation.12 | async-start | bytes 3899392 | tf_op jit(solution)/shard_map/all_gather | solution.py:45
  166.8 2.2 collective-permute-start.6
  203.0 1.6 collective-permute-start.8
  205.5 20.1 %all-to-all-start.6 = ((f32[16,1,64,128]{3,2,1,0:T(8,128)}), f32[16,1,64,128]{3,2,1,0:T(8,128)S(1)}, u32[]{:S(2)}, u32[]{:S(2)}) async-start(f32[16,1,64,128]{3,2,1,0:T(8,128)} %bitcast_bitcast_fusion.7), calls=%async_computation.6 | async-start | bytes 1048576 | tf_op jit(solution)/shard_map/all_to_all | solution.py:40
  226.5 12.4 %all-to-all-start.7 = ((f32[4,4,64,128]{3,2,1,0:T(8,128)}), f32[4,4,64,128]{3,2,1,0:T(8,128)S(1)}, u32[]{:S(2)}, u32[]{:S(2)}) async-start(f32[4,4,64,128]{3,2,1,0:T(8,128)} %broadcast_in_dim.72), calls=%async_computation.7 | async-start | bytes 1048576 | tf_op jit(solution)/shard_map/all_to_all | solution.py:94
  243.3 2.0 collective-permute-start.9
  246.5 22.0 %all-to-all-start.8 = ((f32[16,2,64,128]{3,2,1,0:T(8,128)}), f32[16,2,64,128]{3,2,1,0:T(8,128)S(1)}, u32[]{:S(2)}, u32[]{:S(2)}) async-start(f32[16,2,64,128]{3,2,1,0:T(8,128)} %bitcast_bitcast_fusion.2), calls=%async_computation.8 | async-start | bytes 2097152 | tf_op jit(solution)/shard_map/all_to_all | solution.py:40
  250.1 116.1 %all-gather.8.cloned.1.call-start = ((), (), s32[]{:S(2)}) async-start(), calls=%async_computation.13 | async-start | bytes 3342336 | tf_op jit(solution)/shard_map/all_gather | solution.py:45
  271.0 2.2 collective-permute-start.10
  300.6 1.6 collective-permute-start.11
  319.8 1.6 collective-permute-start.12
  322.3 21.8 %all-to-all-start.11 = ((f32[16,1,64,128]{3,2,1,0:T(8,128)}), f32[16,1,64,128]{3,2,1,0:T(8,128)S(1)}, u32[]{:S(2)}, u32[]{:S(2)}) async-start(f32[16,1,64,128]{3,2,1,0:T(8,128)} %bitcast_bitcast_fusion.5), calls=%async_computation.11 | async-start | bytes 1048576 | tf_op jit(solution)/shard_map/all_to_all | solution.py:40
  366.2 3.1 copy-start.1
Sparse Core Ops, SparseCore 0:
  170.8 63.5 all-gather.5
  294.7 52.8 all-gather.7
